TPU v7x, 32 devices: a whole 2x2x4 slice. The times are simulated.
32 devices in a mesh: dp: 8 (over z, y), feat: 4 (over x, core).
Axes of the slice: x: 2, y: 2, z: 4, core: 2. Of those that a mesh axis runs over, the one named last changes fastest.
Arguments:
- activations: bfloat16 [16384, 2048], P('feat', 'dp'), may hold values from -6 to 6
- cotangent: bfloat16 [16384, 2048], P('feat', 'dp'), may hold values from -6 to 6
- r_mix: bfloat16 [64, 256, 256], P('feat', 'dp'), may hold values from -0.375 to 0.375
- l_mix: bfloat16 [256, 4096], P('feat', 'dp'), may hold values from -0.75 to 0.75
Outputs:
- grad_x: bfloat16 [16384, 2048], P('feat', 'dp')
- grad_r: float32 [64, 256, 256], P('feat', 'dp')
- grad_l: float32 [256, 4096], P('feat', 'dp')
All inputs are finite; a program needn't handle non-finite values.
Results may differ from a plain program's by a relative error of at most 0.0055.
Values may be sent and summed in bfloat16 or wider, within the bound.
No kernel may reach another device: no remote copies, remote signals or barrier semaphores. Data moves between devices by JAX's collectives and lax.ppermute only.
A program may use at most 64 MiB of HBM per device.

v0:
```python
import math
import jax
import jax.numpy as jnp
from jax import lax
from jax.sharding import PartitionSpec as P

BLOCKS = 64
WIDTH = 256


def gelu_tanh(values):
    return jax.nn.gelu(values, approximate=True)


def slope_of(pre_act, upstream):
    _, pullback = jax.vjp(gelu_tanh, pre_act)
    return pullback(upstream.astype(jnp.float32))[0].astype(jnp.bfloat16)


def body(activations, cotangent, r_mix, l_mix):
    tok_count = activations.shape[1]
    local_blocks = activations.shape[0] // WIDTH
    grad_scale = 1.0 / math.sqrt(tok_count * lax.axis_size("dp"))
    r_whole, l_whole = (
        lax.all_gather(r_mix, "dp", axis=1, tiled=True),
        lax.all_gather(l_mix, "dp", axis=1, tiled=True),
    )
    local_cols = l_whole.shape[0]
    l_blocks = l_whole.reshape(local_cols, BLOCKS, BLOCKS)
    x_blocks = activations.reshape(local_blocks, WIDTH, tok_count)
    g_blocks = cotangent.reshape(local_blocks, WIDTH, tok_count)
    mixed_rows = jnp.einsum(
        "bit,bio->bot", x_blocks, r_whole, preferred_element_type=jnp.float32
    ).astype(jnp.bfloat16)
    outgoing = (mixed_rows,)
    parts = (lax.all_to_all(outgoing[0], "feat", split_axis=1, concat_axis=0, tiled=True),)
    columns = parts[0]
    pre_act = jnp.einsum("bst,sbc->cst", columns, l_blocks, preferred_element_type=jnp.float32)
    arrived = (columns, pre_act) + tuple(parts[1:])
    columns = arrived[0]
    pre_act = arrived[1]
    pre_rows = lax.all_to_all(pre_act, "feat", split_axis=0, concat_axis=1, tiled=True)
    slope_rows = slope_of(pre_rows, g_blocks)
    slope_cols = lax.all_to_all(slope_rows, "feat", split_axis=1, concat_axis=0, tiled=True)
    back_cols = jnp.einsum(
        "cst,sbc->bst", slope_cols, l_blocks, preferred_element_type=jnp.float32
    ).astype(jnp.bfloat16)
    l_term = jnp.einsum("bst,cst->sbc", columns, slope_cols, preferred_element_type=jnp.float32)
    l_term = l_term.reshape(local_cols, BLOCKS * BLOCKS) * grad_scale
    back_rows = lax.all_to_all(back_cols, "feat", split_axis=0, concat_axis=1, tiled=True)
    back_rows, through_r = (
        back_rows,
        jnp.einsum("bot,bio->bit", back_rows, r_whole, preferred_element_type=jnp.float32),
    )
    grad_x = (
        (g_blocks.astype(jnp.float32) + through_r)
        .astype(jnp.bfloat16)
        .reshape(local_blocks * WIDTH, tok_count)
    )
    r_term = (
        jnp.einsum("bit,bot->bio", x_blocks, back_rows, preferred_element_type=jnp.float32)
        * grad_scale
    )
    grad_l, grad_r = (
        lax.psum_scatter(l_term, "dp", scatter_dimension=1, tiled=True),
        lax.psum_scatter(r_term, "dp", scatter_dimension=1, tiled=True),
    )
    return (grad_x, grad_r, grad_l)


def solution(mesh):
    placed = (P("feat", "dp"), P("feat", "dp"), P("feat", "dp", None), P("feat", "dp"))
    return jax.shard_map(
        body,
        mesh=mesh,
        in_specs=placed,
        out_specs=(P("feat", "dp"), P("feat", "dp", None), P("feat", "dp")),
        check_vma=False,
    )
```

profile of v0, /device:TPU:0, one launch (start us, length us, event | category | flops | bytes accessed | tf_op | source)
XLA Modules:
  0.0 399.9 jit_solution(9625601833998472881)
XLA Ops:
  7.2 0.7 all-gather.2.cloned.1.call-update
  7.9 54.3 %all-gather.2.cloned.1.call-done = bf16[16,256,256]{2,1,0:T(8,128)(2,1)} async-done(((bf16[16,32,256]{2,1,0:T(8,128)(2,1)}), bf16[16,256,256]{2,1,0:T(8,128)(2,1)}) %all-gather.2.cloned.1.call-update) | async-done | bytes 2097168 | tf_op jit(solution)/shard_map/all_gather | solution.py:25
  62.2 2.4 convolution_convert_fusion
  64.6 2.5 copy.19
  67.1 4.6 %all-to-all-start = ((bf16[16,256,256]{2,0,1:T(8,128)(2,1)}), bf16[16,256,256]{2,0,1:T(8,128)(2,1)}, u32[]{:S(2)}, u32[]{:S(2)}) async-start(bf16[16,256,256]{2,0,1:T(8,128)(2,1)} %copy.19), calls=%async_computation | async-start | bytes 4194304 | tf_op jit(solution)/shard_map/all_to_all | solution.py:36
  71.7 33.3 %all_gather.7 = bf16[64,4096]{1,0:T(8,128)(2,1)} all-gather(bf16[64,512]{1,0:T(8,128)(2,1)S(1)} %copy-done.5), channel_id=1, replica_groups=mesh['dp'=8,'feat'=4] {'dp'}, dimensions={1}, use_global_device_ids=true | all-gather | bytes 589824 | tf_op jit(solution)/shard_map/all_gather | solution.py:26
  105.0 2.1 reshape.22
  107.1 1.8 copy.20
  109.0 1.3 copy-done.1
  110.3 0.8 convolution_bitcast_fusion
  111.0 2.4 copy.22
  113.5 51.1 %all_to_all.72 = f32[64,64,256]{2,1,0:T(8,128)S(1)} all-to-all(f32[64,64,256]{2,1,0:T(8,128)S(1)} %copy.22), channel_id=1, replica_groups=mesh['dp'=8,'feat'=4] {'feat'}, dimensions={0} | all-to-all | bytes 8388608 | tf_op jit(solution)/shard_map/all_to_all | solution.py:42
  164.6 0.5 copy.23
  165.0 1.1 copy-done.4
  166.1 3.3 fusion.6
  169.5 1.2 copy.24
  170.6 28.2 %all_to_all.73 = bf16[16,256,256]{2,0,1:T(8,128)(2,1)S(1)} all-to-all(bf16[16,256,256]{2,0,1:T(8,128)(2,1)S(1)} %copy.24), channel_id=1, replica_groups=mesh['dp'=8,'feat'=4] {'feat'}, dimensions={1} | all-to-all | bytes 4194304 | tf_op jit(solution)/shard_map/all_to_all | solution.py:44
  198.8 0.3 copy.25
  199.1 0.7 convert_bitcast_fusion
  199.8 0.6 copy-done.2
  200.4 1.2 copy.26
  201.6 28.2 %all_to_all.74 = bf16[64,64,256]{2,1,0:T(8,128)(2,1)S(1)} all-to-all(bf16[64,64,256]{2,1,0:T(8,128)(2,1)S(1)} %copy.26), channel_id=1, replica_groups=mesh['dp'=8,'feat'=4] {'feat'}, dimensions={0} | all-to-all | bytes 4194304 | tf_op jit(solution)/shard_map/all_to_all | solution.py:50
  229.8 0.2 copy.27
  230.0 1.3 copy-done.3
  231.4 2.7 multiply_bitcast_fusion
  234.1 5.5 %copy.28 = f32[16,256,256]{2,0,1:T(8,128)} copy(f32[16,256,256]{1,2,0:T(8,128)} %multiply_bitcast_fusion) | data formatting | bytes 8388608 | tf_op jit(solution)/shard_map/mul | solution.py:61
  239.6 4.2 %convolution_multiply_fusion = f32[64,64,64]{2,1,0:T(8,128)} fusion(bf16[64,64,256]{2,0,1:T(8,128)(2,1)} %bitcast.50, bf16[64,64,256]{2,0,1:T(8,128)(2,1)} %bitcast.52), kind=kOutput, calls=%fused_computation.20 | convolution fusion | flops 134479872 | bytes 5242880 | tf_op jit(solution)/shard_map/bst,cst->sbc/dot_general | solution.py:48
  243.9 3.1 mul.78
  247.0 4.9 %fusion.10 = bf16[16,256,256]{2,1,0:T(8,128)(2,1)} fusion(bf16[16,256,256]{2,1,0:T(8,128)(2,1)} %bitcast.58, bf16[16,256,256]{2,1,0:T(8,128)(2,1)} %all-gather.2.cloned.1.call-done, bf16[16,256,256]{2,1,0:T(8,128)(2,1)} %bitcast.54), kind=kOutput, calls=%fused_computation.15 | convolution fusion | flops 540016640 | bytes 8388608 | tf_op jit(solution)/shard_map/bot,bio->bit/dot_general | solution.py:53
  251.9 73.5 %reduce-scatter.3.cloned.1.call-done = f32[16,32,256]{2,0,1:T(8,128)} async-done(((f32[16,256,256]{2,0,1:T(8,128)}), f32[16,32,256]{2,0,1:T(8,128)}) %reduce-scatter.3.cloned.1.call-update) | async-done | bytes 524304 | tf_op jit(solution)/shard_map/reduce_scatter | solution.py:66
  325.4 2.1 copy.29
  327.6 65.8 %reduce-scatter.5.cloned.1.call-done = f32[64,512]{1,0:T(8,128)} async-done(((f32[64,4096]{1,0:T(8,128)}), f32[64,512]{1,0:T(8,128)}) %reduce-scatter.5.cloned.1.call-update) | async-done | bytes 131088 | tf_op jit(solution)/shard_map/reduce_scatter | solution.py:65
  (14 shorter events, 0.2 us)
Async XLA Ops:
  7.2 55.0 %copy-start = (bf16[4096,256]{1,0:T(8,128)(2,1)S(1)}, bf16[4096,256]{1,0:T(8,128)(2,1)}, u32[]{:S(2)}) copy-start(bf16[4096,256]{1,0:T(8,128)(2,1)} %param.4) | copy-start | bytes 6291460
  7.2 55.0 %all-gather.2.cloned.1.call-start = ((), (), s32[]{:S(2)}) async-start(), calls=%async_computation.6 | async-start | bytes 2359296 | tf_op jit(solution)/shard_map/all_gather | solution.py:25
  67.1 4.6 %copy-start.5 = (bf16[64,512]{1,0:T(8,128)(2,1)S(1)}, bf16[64,512]{1,0:T(8,128)(2,1)}, u32[]{:S(2)}) copy-start(bf16[64,512]{1,0:T(8,128)(2,1)} %param.7) | copy-start | bytes 196612
  67.1 40.0 %all-to-all-start = ((bf16[16,256,256]{2,0,1:T(8,128)(2,1)}), bf16[16,256,256]{2,0,1:T(8,128)(2,1)}, u32[]{:S(2)}, u32[]{:S(2)}) async-start(bf16[16,256,256]{2,0,1:T(8,128)(2,1)} %copy.19), calls=%async_computation | async-start | bytes 4194304 | tf_op jit(solution)/shard_map/all_to_all | solution.py:36
  71.6 253.8 %reduce-scatter.3.cloned.1.call-start = ((), (), s32[]{:S(2)}) async-start(), calls=%async_computation.7 | async-start | bytes 4718592 | tf_op jit(solution)/shard_map/reduce_scatter | solution.py:66
  109.0 1.3 copy-start.1
  164.6 1.6 copy-start.4
  199.1 1.3 copy-start.2
  230.0 1.3 copy-start.3
  239.6 153.8 %reduce-scatter.5.cloned.1.call-start = ((), (), s32[]{:S(2)}) async-start(), calls=%async_computation.8 | async-start | bytes 1179648 | tf_op jit(solution)/shard_map/reduce_scatter | solution.py:65
Sparse Core Ops, SparseCore 0:
  10.2 51.9 all-gather.1
  239.7 85.6 reduce-scatter.2
  329.8 63.5 reduce-scatter.4
where the time goes:
time: 401 us; the launch traced here: 400 us
  waiting for transfers between devices  194 us (48%)
  blocking collectives  141 us (35%)
  local copies, waits for them, and re-layouts  27.3 us (7%)
  matrix products  15.7 us (4%)
  between operations  13.9 us (3%)
  starting transfers between devices  4.69 us (1%)
    reduce_scatter x1, waiting for transfers between devices, body(): lax.psum_scatter(r_term, 'dp', scatter_dimension=1, tiled=True)  73.5 us
    reduce_scatter x1, waiting for transfers between devices, body(): lax.psum_scatter(l_term, 'dp', scatter_dimension=1, tiled=True)  65.8 us
    all_gather x1, waiting for transfers between devices, body(): lax.all_gather(r_mix, 'dp', axis=1, tiled=True)  54.3 us
    all_to_all x1, blocking collectives, body(): lax.all_to_all(pre_act, 'feat', split_axis=0, concat_axis=1, tiled=True)  51.1 us
    all_gather x1, blocking collectives, body(): lax.all_gather(l_mix, 'dp', axis=1, tiled=True)  33.3 us
    all_to_all x1, blocking collectives, body(): lax.all_to_all(slope_rows, 'feat', split_axis=1, concat_axis=0, tiled=True)  28.2 us
    all_to_all x1, blocking collectives, body(): lax.all_to_all(back_cols, 'feat', split_axis=0, concat_axis=1, tiled=True)  28.2 us
  transfers between devices with their start and end apart: 4, of which 3 were waited for; matrix products, arithmetic and copies ran while one was open for 4% of the time, Pallas kernels for 0%

commit v1 on v0

--- a/solution.py
+++ b/solution.py
@@ -39,7 +39,10 @@
     arrived = (columns, pre_act) + tuple(parts[1:])
     columns = arrived[0]
     pre_act = arrived[1]
-    pre_rows = lax.all_to_all(pre_act, "feat", split_axis=0, concat_axis=1, tiled=True)
+    pre_rows = jnp.concatenate(
+        lax.all_to_all(jnp.stack(jnp.split(pre_act, lax.axis_size("feat"), axis=0)), "feat", 0, 0),
+        axis=1,
+    )
     slope_rows = slope_of(pre_rows, g_blocks)
     slope_cols = lax.all_to_all(slope_rows, "feat", split_axis=1, concat_axis=0, tiled=True)
     back_cols = jnp.einsum(

time: 401 us -> 400 us (level)
  no operation moved by 1% of the time
where the time goes in v1:
time: 400 us
  waiting for transfers between devices  194 us (48%)
  blocking collectives  141 us (35%)
  local copies, waits for them, and re-layouts  23.9 us (6%)
  matrix products  15.7 us (4%)
  between operations  13.9 us (3%)
  other arithmetic  6.18 us (2%)
  starting transfers between devices  4.71 us (1%)
    reduce_scatter x1, waiting for transfers between devices, body(): lax.psum_scatter(r_term, 'dp', scatter_dimension=1, tiled=True)  73.6 us
    reduce_scatter x1, waiting for transfers between devices, body(): lax.psum_scatter(l_term, 'dp', scatter_dimension=1, tiled=True)  65.9 us
    all_gather x1, waiting for transfers between devices, body(): lax.all_gather(r_mix, 'dp', axis=1, tiled=True)  54.3 us
    all_to_all x1, blocking collectives, body(): lax.all_to_all(jnp.stack(jnp.split(pre_act, lax.axis_size('feat'), axis=0...  51.2 us
    all_gather x1, blocking collectives, body(): lax.all_gather(l_mix, 'dp', axis=1, tiled=True)  33.3 us
    all_to_all x1, blocking collectives, body(): lax.all_to_all(slope_rows, 'feat', split_axis=1, concat_axis=0, tiled=True)  28.2 us
    all_to_all x1, blocking collectives, body(): lax.all_to_all(back_cols, 'feat', split_axis=0, concat_axis=1, tiled=True)  28.2 us
  transfers between devices with their start and end apart: 4, of which 3 were waited for; matrix products, arithmetic and copies ran while one was open for 4% of the time, Pallas kernels for 0%

profile of v1, /device:TPU:0, one launch (start us, length us, event | category | flops | bytes accessed | tf_op | source)
XLA Modules:
  0.0 399.7 jit_solution(11556318988327105060)
XLA Ops:
  7.2 0.7 all-gather.2.cloned.1.call-update
  7.9 54.3 %all-gather.2.cloned.1.call-done = bf16[16,256,256]{2,1,0:T(8,128)(2,1)} async-done(((bf16[16,32,256]{2,1,0:T(8,128)(2,1)}), bf16[16,256,256]{2,1,0:T(8,128)(2,1)}) %all-gather.2.cloned.1.call-update) | async-done | bytes 2097168 | tf_op jit(solution)/shard_map/all_gather | solution.py:25
  62.2 2.4 convolution_convert_fusion
  64.6 2.5 copy.27
  67.1 4.6 %all-to-all-start = ((bf16[16,256,256]{2,0,1:T(8,128)(2,1)}), bf16[16,256,256]{2,0,1:T(8,128)(2,1)}, u32[]{:S(2)}, u32[]{:S(2)}) async-start(bf16[16,256,256]{2,0,1:T(8,128)(2,1)} %copy.27), calls=%async_computation | async-start | bytes 4194304 | tf_op jit(solution)/shard_map/all_to_all | solution.py:36
  71.7 0.0 reduce-scatter.3.cloned.1.call-start
  71.7 33.3 %all_gather.7 = bf16[64,4096]{1,0:T(8,128)(2,1)} all-gather(bf16[64,512]{1,0:T(8,128)(2,1)S(1)} %copy-done.5), channel_id=1, replica_groups=mesh['dp'=8,'feat'=4] {'dp'}, dimensions={1}, use_global_device_ids=true | all-gather | bytes 589824 | tf_op jit(solution)/shard_map/all_gather | solution.py:26
  105.1 2.1 reshape.28
  107.1 1.8 copy.28
  109.0 1.3 copy-done.1
  110.3 0.8 convolution_bitcast_fusion
  111.1 0.6 slice_bitcast_fusion.3
  111.7 0.4 pad_maximum_fusion
  112.1 51.2 %all_to_all.59 = f32[4,16,64,256]{3,1,2,0:T(8,128)S(1)} all-to-all(f32[4,16,64,256]{3,1,2,0:T(8,128)S(1)} %pad_maximum_fusion), channel_id=1, replica_groups=mesh['dp'=8,'feat'=4] {'feat'}, dimensions={0} | all-to-all | bytes 8388608 | tf_op jit(solution)/shard_map/all_to_all | solution.py:43
  163.3 5.7 %fusion.6 = bf16[16,256,256]{2,1,0:T(8,128)(2,1)S(1)} fusion(bf16[16,256,256]{2,1,0:T(8,128)(2,1)S(1)} %bitcast.59, f32[16,256,256]{2,0,1:T(8,128)S(1)} %bitcast.55), kind=kLoop, calls=%fused_computation.11 | loop fusion | flops 22020096 | bytes 8388608 | tf_op jit(solution)/shard_map/convert_element_type | solution.py:17
  169.1 1.2 copy.35
  170.3 28.2 %all_to_all.60 = bf16[16,256,256]{2,0,1:T(8,128)(2,1)S(1)} all-to-all(bf16[16,256,256]{2,0,1:T(8,128)(2,1)S(1)} %copy.35), channel_id=1, replica_groups=mesh['dp'=8,'feat'=4] {'feat'}, dimensions={1} | all-to-all | bytes 4194304 | tf_op jit(solution)/shard_map/all_to_all | solution.py:47
  198.4 0.3 copy.36
  198.7 0.7 convert_bitcast_fusion
  199.4 0.6 copy-done.2
  200.0 1.2 copy.37
  201.2 28.2 %all_to_all.61 = bf16[64,64,256]{2,1,0:T(8,128)(2,1)S(1)} all-to-all(bf16[64,64,256]{2,1,0:T(8,128)(2,1)S(1)} %copy.37), channel_id=1, replica_groups=mesh['dp'=8,'feat'=4] {'feat'}, dimensions={0} | all-to-all | bytes 4194304 | tf_op jit(solution)/shard_map/all_to_all | solution.py:53
  229.4 0.2 copy.38
  229.7 1.3 copy-done.3
  231.0 2.7 multiply_bitcast_fusion
  233.7 5.5 %copy.39 = f32[16,256,256]{2,0,1:T(8,128)} copy(f32[16,256,256]{1,2,0:T(8,128)} %multiply_bitcast_fusion) | data formatting | bytes 8388608 | tf_op jit(solution)/shard_map/mul | solution.py:64
  239.2 4.2 %convolution_multiply_fusion = f32[64,64,64]{2,1,0:T(8,128)} fusion(bf16[64,64,256]{2,0,1:T(8,128)(2,1)} %bitcast.50, bf16[64,64,256]{2,0,1:T(8,128)(2,1)} %bitcast.52), kind=kOutput, calls=%fused_computation.21 | convolution fusion | flops 134479872 | bytes 5242880 | tf_op jit(solution)/shard_map/bst,cst->sbc/dot_general | solution.py:51
  243.5 3.1 mul.78
  246.6 4.9 %fusion.10 = bf16[16,256,256]{2,1,0:T(8,128)(2,1)} fusion(bf16[16,256,256]{2,1,0:T(8,128)(2,1)} %bitcast.58, bf16[16,256,256]{2,1,0:T(8,128)(2,1)} %all-gather.2.cloned.1.call-done, bf16[16,256,256]{2,1,0:T(8,128)(2,1)} %bitcast.54), kind=kOutput, calls=%fused_computation.15 | convolution fusion | flops 540016640 | bytes 8388608 | tf_op jit(solution)/shard_map/bot,bio->bit/dot_general | solution.py:56
  251.5 73.6 %reduce-scatter.3.cloned.1.call-done = f32[16,32,256]{2,0,1:T(8,128)} async-done(((f32[16,256,256]{2,0,1:T(8,128)}), f32[16,32,256]{2,0,1:T(8,128)}) %reduce-scatter.3.cloned.1.call-update) | async-done | bytes 524304 | tf_op jit(solution)/shard_map/reduce_scatter | solution.py:69
  325.1 2.1 copy.40
  327.2 65.9 %reduce-scatter.5.cloned.1.call-done = f32[64,512]{1,0:T(8,128)} async-done(((f32[64,4096]{1,0:T(8,128)}), f32[64,512]{1,0:T(8,128)}) %reduce-scatter.5.cloned.1.call-update) | async-done | bytes 131088 | tf_op jit(solution)/shard_map/reduce_scatter | solution.py:68
  (14 shorter events, 0.1 us)
Async XLA Ops:
  7.2 55.0 %copy-start = (bf16[4096,256]{1,0:T(8,128)(2,1)S(1)}, bf16[4096,256]{1,0:T(8,128)(2,1)}, u32[]{:S(2)}) copy-start(bf16[4096,256]{1,0:T(8,128)(2,1)} %param.4) | copy-start | bytes 6291460
  7.2 55.0 %all-gather.2.cloned.1.call-start = ((), (), s32[]{:S(2)}) async-start(), calls=%async_computation.6 | async-start | bytes 2359296 | tf_op jit(solution)/shard_map/all_gather | solution.py:25
  67.1 4.7 %copy-start.5 = (bf16[64,512]{1,0:T(8,128)(2,1)S(1)}, bf16[64,512]{1,0:T(8,128)(2,1)}, u32[]{:S(2)}) copy-start(bf16[64,512]{1,0:T(8,128)(2,1)} %param.7) | copy-start | bytes 196612
  67.1 40.1 %all-to-all-start = ((bf16[16,256,256]{2,0,1:T(8,128)(2,1)}), bf16[16,256,256]{2,0,1:T(8,128)(2,1)}, u32[]{:S(2)}, u32[]{:S(2)}) async-start(bf16[16,256,256]{2,0,1:T(8,128)(2,1)} %copy.27), calls=%async_computation | async-start | bytes 4194304 | tf_op jit(solution)/shard_map/all_to_all | solution.py:36
  71.7 253.4 %reduce-scatter.3.cloned.1.call-start = ((), (), s32[]{:S(2)}) async-start(), calls=%async_computation.7 | async-start | bytes 4718592 | tf_op jit(solution)/shard_map/reduce_scatter | solution.py:69
  109.0 1.3 copy-start.1
  112.1 51.2 %copy-start.4 = (bf16[4096,256]{1,0:T(8,128)(2,1)S(1)}, bf16[4096,256]{1,0:T(8,128)(2,1)}, u32[]{:S(2)}) copy-start(bf16[4096,256]{1,0:T(8,128)(2,1)} %param.5) | copy-start | bytes 6291460
  198.7 1.3 copy-start.2
  229.6 1.3 copy-start.3
  239.2 154.0 %reduce-scatter.5.cloned.1.call-start = ((), (), s32[]{:S(2)}) async-start(), calls=%async_computation.8 | async-start | bytes 1179648 | tf_op jit(solution)/shard_map/reduce_scatter | solution.py:68
Sparse Core Ops, SparseCore 0:
  10.2 51.9 all-gather.1
  239.3 85.7 reduce-scatter.2
  329.5 63.6 reduce-scatter.4
